TPU v7x, 32 devices: a whole 2x2x4 slice. The times are simulated.
32 devices in a mesh: rep: 2 (over y), ctx: 8 (over z, x), head: 2 (over core).
Axes of the slice: x: 2, y: 2, z: 4, core: 2. Of those that a mesh axis runs over, the one named last changes fastest.
Arguments:
- queries: bfloat16 [1024, 32, 128], P(('rep', 'ctx'), 'head'), parts along dimension 0, may hold values from -6 to 6
- keys: bfloat16 [1024, 4, 128], P(('rep', 'ctx'), 'head'), parts along dimension 0, may hold values from -6 to 6
- values: bfloat16 [1024, 4, 128], P(('rep', 'ctx'), 'head'), parts along dimension 0, may hold values from -6 to 6
Outputs:
- attended: bfloat16 [1024, 32, 128], P(('rep', 'ctx'), 'head'), parts along dimension 0
There are 2 independent parts, one for each index of `rep`. A program takes and returns all parts, laid end to end along the dimension named above; each array names one. Nothing has to cross between parts.
All inputs are finite; a program needn't handle non-finite values.
Results may differ from a plain program's by a relative error of at most 0.0037.
Values may be sent and summed in bfloat16 or wider, within the bound.
No kernel may reach another device: no remote copies, remote signals or barrier semaphores. Data moves between devices by JAX's collectives and lax.ppermute only.
A program may use at most 128 MiB of HBM per device.

v0:
```python
import jax
import jax.numpy as jnp
from jax import lax
from jax.sharding import PartitionSpec as P


def from_partner(x, axis, bit):
    return lax.ppermute(x, axis, [(i, i ^ 1 << bit) for i in range(lax.axis_size(axis))])


def attend_piece(state, rows, position, key_piece, value_piece, scale):
    running_max, running_sum, weighted = state
    scores = (
        jnp.einsum("qhgd,khd->hgqk", rows, key_piece, preferred_element_type=jnp.float32) * scale
    )
    key_position = jnp.arange(key_piece.shape[0], dtype=jnp.int32)
    valid = key_position[None, :] <= position[:, None]
    scores = jnp.where(valid, scores, -1e30)
    new_max = jnp.maximum(running_max, jnp.max(scores, axis=-1))
    weights = jnp.where(valid, jnp.exp(scores - new_max[..., None]), 0.0)
    running_sum = jnp.sum(weights, axis=-1)
    update = jnp.einsum(
        "hgqk,khd->hgqd",
        weights.astype(jnp.bfloat16),
        value_piece,
        preferred_element_type=jnp.float32,
    )
    weighted = update
    return (new_max, running_sum, weighted)


def finish(state, half_rows, query_heads, head_size):
    running_max, running_sum, weighted = state
    result = weighted / running_sum[..., None]
    result = jnp.transpose(result, (2, 0, 1, 3)).reshape(half_rows, query_heads, head_size)
    return result.astype(jnp.bfloat16)


def per_device(queries, keys, values):
    local_rows, query_heads, head_size = queries.shape
    key_heads = keys.shape[1]
    group_size = query_heads // key_heads
    half_rows = local_rows // 2
    scale = head_size ** (-0.5)
    context_size = lax.axis_size("ctx")
    position_index = lax.axis_index("ctx")
    offset = jnp.arange(half_rows, dtype=jnp.int32)
    first_rows = queries[:half_rows]
    first_position = position_index * local_rows + offset
    second_rows = queries[half_rows:]
    bit_count = context_size.bit_length() - 1
    for bit_index in range(bit_count):
        second_rows = from_partner(second_rows, "ctx", bit_index)
    second_position = (context_size - 1 - position_index) * local_rows + half_rows + offset
    halves = (
        (first_rows.reshape(half_rows, key_heads, group_size, head_size), first_position),
        (second_rows.reshape(half_rows, key_heads, group_size, head_size), second_position),
    )
    initial = (
        jnp.full((key_heads, group_size, half_rows), -1e30, jnp.float32),
        jnp.zeros((key_heads, group_size, half_rows), jnp.float32),
        jnp.zeros((key_heads, group_size, half_rows, head_size), jnp.float32),
    )
    carries = (initial, initial)
    start = jnp.int32(0)
    key_piece = lax.all_gather(keys, "ctx", axis=0, tiled=True)
    value_piece = lax.all_gather(values, "ctx", axis=0, tiled=True)
    updated = []
    for which in range(2):
        rows, position = halves[which]
        needed = start <= position[-1]
        updated.append(
            lax.cond(
                needed,
                lambda state: attend_piece(state, rows, position, key_piece, value_piece, scale),
                lambda state: state,
                carries[which],
            )
        )
    carries = (updated[0], updated[1])
    first_out = finish(carries[0], half_rows, query_heads, head_size)
    second_out = finish(carries[1], half_rows, query_heads, head_size)
    for bit_index in range(bit_count):
        second_out = from_partner(second_out, "ctx", bit_index)
    return jnp.concatenate([first_out, second_out], axis=0)


def solution(mesh):
    placed = (
        P(("rep", "ctx"), "head", None),
        P(("rep", "ctx"), "head", None),
        P(("rep", "ctx"), "head", None),
    )
    return jax.shard_map(
        per_device,
        mesh=mesh,
        in_specs=placed,
        out_specs=P(("rep", "ctx"), "head", None),
        check_vma=False,
    )
```

profile of v0, /device:TPU:0, one launch (start us, length us, event | category | flops | bytes accessed | tf_op | source)
XLA Modules:
  0.0 91.4 jit_solution(11736791477938292127)
XLA Ops:
  0.0 0.9 slice-done
  0.9 3.0 %collective-permute-start = (bf16[32,16,128]{2,0,1:T(8,128)(2,1)S(1)}, bf16[32,16,128]{2,0,1:T(8,128)(2,1)S(1)}, u32[]{:S(2)}, u32[]{:S(2)}) collective-permute-start(bf16[32,16,128]{2,0,1:T(8,128)(2,1)S(1)} %copy.14), channel_id=1, source_target_pairs={{0,2},{2,0},{4,6},{6,4},{8,10},{10,8},{12,14},{14,12},{1,3},{3,1},... | collective-permute-start | bytes 393224 | tf_op jit(solution)/shard_map/ppermute | solution.py:8
  4.0 3.5 %collective-permute-done = bf16[32,16,128]{2,0,1:T(8,128)(2,1)S(1)} collective-permute-done((bf16[32,16,128]{2,0,1:T(8,128)(2,1)S(1)}, bf16[32,16,128]{2,0,1:T(8,128)(2,1)S(1)}, u32[]{:S(2)}, u32[]{:S(2)}) %collective-permute-start) | collective-permute-done | bytes 131104 | tf_op jit(solution)/shard_map/ppermute | solution.py:8
  7.5 1.8 %collective-permute-start.1 = (bf16[32,16,128]{2,0,1:T(8,128)(2,1)S(1)}, bf16[32,16,128]{2,0,1:T(8,128)(2,1)S(1)}, u32[]{:S(2)}, u32[]{:S(2)}) collective-permute-start(bf16[32,16,128]{2,0,1:T(8,128)(2,1)S(1)} %collective-permute-done), channel_id=1, source_target_pairs={{0,4},{2,6},{4,0},{6,2},{8,12},{10,14},{12,8},{14,10},{1,5},{3,7},... | collective-permute-start | bytes 393224 | tf_op jit(solution)/shard_map/ppermute | solution.py:8
  9.3 0.0 copy-start.2
  9.3 31.0 %all_gather.6 = bf16[512,2,128]{2,0,1:T(8,128)(2,1)S(1)} all-gather(bf16[64,2,128]{2,0,1:T(8,128)(2,1)S(1)} %copy.4), channel_id=1, replica_groups=mesh['rep'=2,'ctx'=8,'head'=2] {'ctx'}, dimensions={0}, use_global_device_ids=true | all-gather | bytes 294912 | tf_op jit(solution)/shard_map/all_gather | solution.py:66
  40.4 0.6 slice.14
  41.6 31.0 %all_gather.7 = bf16[512,2,128]{2,0,1:T(8,128)(2,1)S(1)} all-gather(bf16[64,2,128]{2,0,1:T(8,128)(2,1)S(1)} %copy.5), channel_id=1, replica_groups=mesh['rep'=2,'ctx'=8,'head'=2] {'ctx'}, dimensions={0}, use_global_device_ids=true | all-gather | bytes 294912 | tf_op jit(solution)/shard_map/all_gather | solution.py:67
  72.6 0.0 collective-permute-done.2
  72.6 1.2 %conditional.3 = (f32[2,8,32]{2,1,0:T(8,128)S(1)}, f32[2,8,32,128]{3,2,1,0:T(8,128)S(1)}) conditional(s32[]{:T(128)} %bitcast.15, () %tuple.23, (s32[32]{0:T(128)S(1)}, bf16[32,16,128]{2,0,1:T(8,128)(2,1)S(1)}, bf16[512,2,128]{2,0,1:T(8,128)(2,1)S(1)}, bf16[512,2,128]{2,0,1:T(8,128)(2,1)S(1)}) %tuple.24), branch_computations={%region_4.5_spmd, %region_5.8_spmd} | conditional | flops 136592896 | bytes 4141200 | solution.py:73
  72.6 0.1 iota_compare_fusion.1
  72.7 0.4 fusion.27
  73.1 0.4 fusion.16
  73.4 0.3 fusion.15
  73.8 0.0 copy-start
  73.8 0.1 fusion.25
  73.9 0.1 copy.17
  74.0 0.8 collective-permute-start.3
  74.8 4.2 %collective-permute-done.3 = bf16[32,16,128]{2,1,0:T(8,128)(2,1)S(1)} collective-permute-done((bf16[32,16,128]{2,1,0:T(8,128)(2,1)S(1)}, bf16[32,16,128]{2,1,0:T(8,128)(2,1)S(1)}, u32[]{:S(2)}, u32[]{:S(2)}) %collective-permute-start.3) | collective-permute-done | bytes 131104 | tf_op jit(solution)/shard_map/ppermute | solution.py:8
  79.0 0.6 slice.13
  80.3 1.3 %conditional.2 = (f32[2,8,32]{2,1,0:T(8,128)S(1)}, f32[2,8,32,128]{3,2,1,0:T(8,128)S(1)}) conditional(s32[]{:T(128)} %bitcast.12, () %tuple.21, (s32[32]{0:T(128)S(1)}, bf16[64,16,128]{2,1,0:T(8,128)(2,1)S(1)}, bf16[512,2,128]{2,0,1:T(8,128)(2,1)S(1)}, bf16[512,2,128]{2,0,1:T(8,128)(2,1)S(1)}) %tuple.32), branch_computations={%region_0.0_spmd, %region_1.4_spmd} | conditional | flops 136592896 | bytes 4927632 | solution.py:73
  80.3 0.1 iota_compare_fusion
  80.4 0.1 copy.6
  80.5 0.4 fusion.26
  80.9 0.4 fusion.4
  81.2 0.3 fusion.3
  81.6 2.4 %collective-permute-done.4 = bf16[32,16,128]{2,1,0:T(8,128)(2,1)S(1)} collective-permute-done((bf16[32,16,128]{2,1,0:T(8,128)(2,1)S(1)}, bf16[32,16,128]{2,1,0:T(8,128)(2,1)S(1)}, u32[]{:S(2)}, u32[]{:S(2)}) %collective-permute-start.4) | collective-permute-done | bytes 131104 | tf_op jit(solution)/shard_map/ppermute | solution.py:8
  84.0 0.7 collective-permute-start.5
  84.7 0.1 fusion.24
  84.8 0.1 copy.18
  84.9 5.8 %collective-permute-done.5 = bf16[32,16,128]{2,1,0:T(8,128)(2,1)S(1)} collective-permute-done((bf16[32,16,128]{2,1,0:T(8,128)(2,1)S(1)}, bf16[32,16,128]{2,1,0:T(8,128)(2,1)S(1)}, u32[]{:S(2)}, u32[]{:S(2)}) %collective-permute-start.5) | collective-permute-done | bytes 131104 | tf_op jit(solution)/shard_map/ppermute | solution.py:8
  90.7 0.7 pad_maximum_fusion
  (16 shorter events, 0.1 us)
Async XLA Ops:
  0.0 0.9 slice-start
  0.9 8.4 %copy-start.1 = (bf16[64,2,128]{2,1,0:T(2,128)(2,1)S(1)}, bf16[64,2,128]{2,1,0:T(2,128)(2,1)}, u32[]{:S(2)}) copy-start(bf16[64,2,128]{2,1,0:T(2,128)(2,1)} %param.8) | copy-start | bytes 98308
  0.9 6.5 %collective-permute-start = (bf16[32,16,128]{2,0,1:T(8,128)(2,1)S(1)}, bf16[32,16,128]{2,0,1:T(8,128)(2,1)S(1)}, u32[]{:S(2)}, u32[]{:S(2)}) collective-permute-start(bf16[32,16,128]{2,0,1:T(8,128)(2,1)S(1)} %copy.14), channel_id=1, source_target_pairs={{0,2},{2,0},{4,6},{6,4},{8,10},{10,8},{12,14},{14,12},{1,3},{3,1},... | collective-permute-start | bytes 393224 | tf_op jit(solution)/shard_map/ppermute | solution.py:8
  7.5 32.9 %collective-permute-start.1 = (bf16[32,16,128]{2,0,1:T(8,128)(2,1)S(1)}, bf16[32,16,128]{2,0,1:T(8,128)(2,1)S(1)}, u32[]{:S(2)}, u32[]{:S(2)}) collective-permute-start(bf16[32,16,128]{2,0,1:T(8,128)(2,1)S(1)} %collective-permute-done), channel_id=1, source_target_pairs={{0,4},{2,6},{4,0},{6,2},{8,12},{10,14},{12,8},{14,10},{1,5},{3,7},... | collective-permute-start | bytes 393224 | tf_op jit(solution)/shard_map/ppermute | solution.py:8
  9.3 31.0 %copy-start.2 = (bf16[64,2,128]{2,1,0:T(2,128)(2,1)S(1)}, bf16[64,2,128]{2,1,0:T(2,128)(2,1)}, u32[]{:S(2)}) copy-start(bf16[64,2,128]{2,1,0:T(2,128)(2,1)} %param.9) | copy-start | bytes 98308
  40.4 32.2 %collective-permute-start.2 = (bf16[32,16,128]{2,0,1:T(8,128)(2,1)S(1)}, bf16[32,16,128]{2,0,1:T(8,128)(2,1)S(1)}, u32[]{:S(2)}, u32[]{:S(2)}) collective-permute-start(bf16[32,16,128]{2,0,1:T(8,128)(2,1)S(1)} %collective-permute-done.1), channel_id=1, source_target_pairs={{0,8},{2,10},{4,12},{6,14},{8,0},{10,2},{12,4},{14,6},{1,9},{3,11}... | collective-permute-start | bytes 393224 | tf_op jit(solution)/shard_map/ppermute | solution.py:8
  73.8 6.5 %copy-start = (bf16[64,16,128]{2,1,0:T(8,128)(2,1)S(1)}, bf16[64,16,128]{2,1,0:T(8,128)(2,1)}, u32[]{:S(2)}) copy-start(bf16[64,16,128]{2,1,0:T(8,128)(2,1)} %param.7) | copy-start | bytes 786436
  74.0 5.0 %collective-permute-start.3 = (bf16[32,16,128]{2,1,0:T(8,128)(2,1)S(1)}, bf16[32,16,128]{2,1,0:T(8,128)(2,1)S(1)}, u32[]{:S(2)}, u32[]{:S(2)}) collective-permute-start(bf16[32,16,128]{2,1,0:T(8,128)(2,1)S(1)} %bitcast.51), channel_id=1, source_target_pairs={{0,2},{2,0},{4,6},{6,4},{8,10},{10,8},{12,14},{14,12},{1,3},{3,1},... | collective-permute-start | bytes 393224 | tf_op jit(solution)/shard_map/ppermute | solution.py:8
  79.0 5.0 %collective-permute-start.4 = (bf16[32,16,128]{2,1,0:T(8,128)(2,1)S(1)}, bf16[32,16,128]{2,1,0:T(8,128)(2,1)S(1)}, u32[]{:S(2)}, u32[]{:S(2)}) collective-permute-start(bf16[32,16,128]{2,1,0:T(8,128)(2,1)S(1)} %collective-permute-done.3), channel_id=1, source_target_pairs={{0,4},{2,6},{4,0},{6,2},{8,12},{10,14},{12,8},{14,10},{1,5},{3,7},... | collective-permute-start | bytes 393224 | tf_op jit(solution)/shard_map/ppermute | solution.py:8
  84.0 6.7 %collective-permute-start.5 = (bf16[32,16,128]{2,1,0:T(8,128)(2,1)S(1)}, bf16[32,16,128]{2,1,0:T(8,128)(2,1)S(1)}, u32[]{:S(2)}, u32[]{:S(2)}) collective-permute-start(bf16[32,16,128]{2,1,0:T(8,128)(2,1)S(1)} %collective-permute-done.4), channel_id=1, source_target_pairs={{0,8},{2,10},{4,12},{6,14},{8,0},{10,2},{12,4},{14,6},{1,9},{3,11}... | collective-permute-start | bytes 393224 | tf_op jit(solution)/shard_map/ppermute | solution.py:8
where the time goes:
time: 91.6 us; the launch traced here: 91.4 us
  blocking collectives  62 us (68%)
  waiting for transfers between devices  15.9 us (17%)
  starting transfers between devices  6.41 us (7%)
  local copies, waits for them, and re-layouts  2.32 us (3%)
  other arithmetic  1.85 us (2%)
  matrix products  1.47 us (2%)
  between operations  1.41 us (2%)
    all_gather x1, blocking collectives, per_device(): key_piece = lax.all_gather(keys, 'ctx', axis=0, tiled=True)  31 us
    all_gather x1, blocking collectives, per_device(): value_piece = lax.all_gather(values, 'ctx', axis=0, tiled=True)  31 us
    ppermute x6, waiting for transfers between devices, from_partner(): lax.ppermute(x, axis, [(i, i ^ 1 << bit) for i in range(lax.axis_size(axi...  15.9 us
    ppermute x6, starting transfers between devices, from_partner(): lax.ppermute(x, axis, [(i, i ^ 1 << bit) for i in range(lax.axis_size(axi...  6.41 us
  transfers between devices with their start and end apart: 6, of which 4 were waited for; matrix products, arithmetic and copies ran while one was open for 3% of the time, Pallas kernels for 0%

commit v1 on v0

--- a/solution.py
+++ b/solution.py
@@ -63,7 +63,14 @@
     )
     carries = (initial, initial)
     start = jnp.int32(0)
-    key_piece = lax.all_gather(keys, "ctx", axis=0, tiled=True)
+    ways, here, turn = (lax.axis_size("ctx"), lax.axis_index("ctx"), keys.shape[0])
+    line, have = (keys, 1)
+    while have < ways:
+        line = jnp.concatenate(
+            [line, lax.ppermute(line, "ctx", [(d, (d - have) % ways) for d in range(ways)])], axis=0
+        )
+        have = 2 * have
+    key_piece = jnp.roll(line, here * turn, axis=0)
     value_piece = lax.all_gather(values, "ctx", axis=0, tiled=True)
     updated = []
     for which in range(2):

time: 91.6 us -> 76.3 us (0.83)
  blocking collectives: 62 us -> 31.1 us
  waiting for transfers between devices: 15.9 us -> 24.4 us
  starting transfers between devices: 6.41 us -> 13.3 us
    all_gather x1 -> x0, blocking collectives: 31 us -> none  [per_device(): key_piece = lax.all_gather(keys, 'ctx', axis=0, tiled=True)]
    ppermute x0 -> x3, starting transfers between devices: none -> 6.49 us  [per_device(): lax.ppermute(line, 'ctx', [(d, (d - have) % ways) for d in range(ways)])]
    ppermute x0 -> x3, waiting for transfers between devices: none -> 5.91 us  [per_device(): lax.ppermute(line, 'ctx', [(d, (d - have) % ways) for d in range(ways)])]
    ppermute x6, waiting for transfers between devices: 15.9 us -> 18.5 us  [from_partner(): lax.ppermute(x, axis, [(i, i ^ 1 << bit) for i in range(lax.axis_size(axi...]
  transfers between devices with their start and end apart: 6 -> 9, of which waited for: 4 -> 7; matrix products, arithmetic and copies ran while one was open for 3% -> 4% of each run, Pallas kernels for 0% -> 0%
where the time goes in v1:
time: 76.3 us; the launch traced here: 76.1 us
  blocking collectives  31.1 us (41%)
  waiting for transfers between devices  24.4 us (32%)
  starting transfers between devices  13.3 us (17%)
  local copies, waits for them, and re-layouts  2.46 us (3%)
  other arithmetic  1.87 us (2%)
  between operations  1.49 us (2%)
  matrix products  1.47 us (2%)
    all_gather x1, blocking collectives, per_device(): value_piece = lax.all_gather(values, 'ctx', axis=0, tiled=True)  31.1 us
    ppermute x6, waiting for transfers between devices, from_partner(): lax.ppermute(x, axis, [(i, i ^ 1 << bit) for i in range(lax.axis_size(axi...  18.5 us
    ppermute x6, starting transfers between devices, from_partner(): lax.ppermute(x, axis, [(i, i ^ 1 << bit) for i in range(lax.axis_size(axi...  6.79 us
    ppermute x3, starting transfers between devices, per_device(): lax.ppermute(line, 'ctx', [(d, (d - have) % ways) for d in range(ways)])  6.49 us
    ppermute x3, waiting for transfers between devices, per_device(): lax.ppermute(line, 'ctx', [(d, (d - have) % ways) for d in range(ways)])  5.91 us
  transfers between devices with their start and end apart: 9, of which 7 were waited for; matrix products, arithmetic and copies ran while one was open for 4% of the time, Pallas kernels for 0%

profile of v1, /device:TPU:0, one launch (start us, length us, event | category | flops | bytes accessed | tf_op | source)
XLA Modules:
  0.0 76.1 jit_solution(13497617495609813109)
XLA Ops:
  0.0 0.9 %slice-done = bf16[32,16,128]{2,1,0:T(8,128)(2,1)S(1)} async-done(((bf16[64,16,128]{2,1,0:T(8,128)(2,1)}), bf16[32,16,128]{2,1,0:T(8,128)(2,1)S(1)}, s32[]{:S(2)}) %slice-start) | async-done | bytes 131096 | tf_op jit(solution)/shard_map/slice | solution.py:50
  0.9 3.0 %collective-permute-start.3 = (bf16[32,16,128]{2,0,1:T(8,128)(2,1)S(1)}, bf16[32,16,128]{2,0,1:T(8,128)(2,1)S(1)}, u32[]{:S(2)}, u32[]{:S(2)}) collective-permute-start(bf16[32,16,128]{2,0,1:T(8,128)(2,1)S(1)} %copy.18), channel_id=1, source_target_pairs={{0,2},{2,0},{4,6},{6,4},{8,10},{10,8},{12,14},{14,12},{1,3},{3,1},... | collective-permute-start | bytes 393224 | tf_op jit(solution)/shard_map/ppermute | solution.py:8
  4.0 3.7 %collective-permute-start = (bf16[64,2,128]{2,0,1:T(8,128)(2,1)S(1)}, bf16[64,2,128]{2,0,1:T(8,128)(2,1)S(1)}, u32[]{:S(2)}, u32[]{:S(2)}) collective-permute-start(bf16[64,2,128]{2,0,1:T(8,128)(2,1)S(1)} %get-tuple-element.48), channel_id=1, source_target_pairs={{0,14},{2,0},{4,2},{6,4},{8,6},{10,8},{12,10},{14,12},{1,15},{3,1}... | collective-permute-start | bytes 98312 | tf_op jit(solution)/shard_map/ppermute | solution.py:70
  7.8 0.6 slice.14
  9.0 0.3 collective-permute-done
  9.4 2.7 %collective-permute-start.1 = (bf16[128,2,128]{2,0,1:T(8,128)(2,1)S(1)}, bf16[128,2,128]{2,0,1:T(8,128)(2,1)S(1)}, u32[]{:S(2)}, u32[]{:S(2)}) collective-permute-start(bf16[128,2,128]{2,0,1:T(8,128)(2,1)S(1)} %pad_maximum_fusion.2), channel_id=1, source_target_pairs={{0,12},{2,14},{4,0},{6,2},{8,4},{10,6},{12,8},{14,10},{1,13},{3,15... | collective-permute-start | bytes 196616 | tf_op jit(solution)/shard_map/ppermute | solution.py:70
  12.0 31.1 %all_gather.3 = bf16[512,2,128]{2,0,1:T(8,128)(2,1)S(1)} all-gather(bf16[64,2,128]{2,0,1:T(8,128)(2,1)S(1)} %copy.9), channel_id=1, replica_groups=mesh['rep'=2,'ctx'=8,'head'=2] {'ctx'}, dimensions={0}, use_global_device_ids=true | all-gather | bytes 294912 | tf_op jit(solution)/shard_map/all_gather | solution.py:74
  43.1 0.1 collective-permute-start.2
  43.3 1.2 %collective-permute-start.4 = (bf16[32,16,128]{2,0,1:T(8,128)(2,1)S(1)}, bf16[32,16,128]{2,0,1:T(8,128)(2,1)S(1)}, u32[]{:S(2)}, u32[]{:S(2)}) collective-permute-start(bf16[32,16,128]{2,0,1:T(8,128)(2,1)S(1)} %collective-permute-done.3), channel_id=1, source_target_pairs={{0,4},{2,6},{4,0},{6,2},{8,12},{10,14},{12,8},{14,10},{1,5},{3,7},... | collective-permute-start | bytes 393224 | tf_op jit(solution)/shard_map/ppermute | solution.py:8
  44.4 5.6 %collective-permute-done.2 = bf16[256,2,128]{2,0,1:T(8,128)(2,1)S(1)} collective-permute-done((bf16[256,2,128]{2,0,1:T(8,128)(2,1)S(1)}, bf16[256,2,128]{2,0,1:T(8,128)(2,1)S(1)}, u32[]{:S(2)}, u32[]{:S(2)}) %collective-permute-start.2) | collective-permute-done | bytes 131104 | tf_op jit(solution)/shard_map/ppermute | solution.py:70
  50.1 0.9 %collective-permute-done.4 = bf16[32,16,128]{2,0,1:T(8,128)(2,1)S(1)} collective-permute-done((bf16[32,16,128]{2,0,1:T(8,128)(2,1)S(1)}, bf16[32,16,128]{2,0,1:T(8,128)(2,1)S(1)}, u32[]{:S(2)}, u32[]{:S(2)}) %collective-permute-start.4) | collective-permute-done | bytes 131104 | tf_op jit(solution)/shard_map/ppermute | solution.py:8
  51.0 0.2 collective-permute-start.5
  51.2 6.0 %collective-permute-done.5 = bf16[32,16,128]{2,0,1:T(8,128)(2,1)S(1)} collective-permute-done((bf16[32,16,128]{2,0,1:T(8,128)(2,1)S(1)}, bf16[32,16,128]{2,0,1:T(8,128)(2,1)S(1)}, u32[]{:S(2)}, u32[]{:S(2)}) %collective-permute-start.5) | collective-permute-done | bytes 131104 | tf_op jit(solution)/shard_map/ppermute | solution.py:8
  57.2 1.2 %conditional.3 = (f32[2,8,32]{2,1,0:T(8,128)S(1)}, f32[2,8,32,128]{3,2,1,0:T(8,128)S(1)}) conditional(s32[]{:T(128)} %bitcast.15, () %tuple.23, (s32[32]{0:T(128)S(1)}, bf16[32,16,128]{2,0,1:T(8,128)(2,1)S(1)}, bf16[512,2,128]{2,0,1:T(8,128)(2,1)S(1)}, bf16[512,2,128]{2,0,1:T(8,128)(2,1)S(1)}) %tuple.24), branch_computations={%region_4.5_spmd, %region_5.8_spmd} | conditional | flops 136592896 | bytes 4141200 | solution.py:80
  57.2 0.1 iota_compare_fusion.1
  57.3 0.4 fusion.27
  57.7 0.3 fusion.15
  58.1 0.4 fusion.16
  58.4 0.1 fusion.25
  58.6 1.8 %collective-permute-start.6 = (bf16[32,16,128]{2,1,0:T(8,128)(2,1)S(1)}, bf16[32,16,128]{2,1,0:T(8,128)(2,1)S(1)}, u32[]{:S(2)}, u32[]{:S(2)}) collective-permute-start(bf16[32,16,128]{2,1,0:T(8,128)(2,1)S(1)} %bitcast.51), channel_id=1, source_target_pairs={{0,2},{2,0},{4,6},{6,4},{8,10},{10,8},{12,14},{14,12},{1,3},{3,1},... | collective-permute-start | bytes 393224 | tf_op jit(solution)/shard_map/ppermute | solution.py:8
  60.4 3.3 %collective-permute-done.6 = bf16[32,16,128]{2,1,0:T(8,128)(2,1)S(1)} collective-permute-done((bf16[32,16,128]{2,1,0:T(8,128)(2,1)S(1)}, bf16[32,16,128]{2,1,0:T(8,128)(2,1)S(1)}, u32[]{:S(2)}, u32[]{:S(2)}) %collective-permute-start.6) | collective-permute-done | bytes 131104 | tf_op jit(solution)/shard_map/ppermute | solution.py:8
  63.7 0.6 slice.13
  64.9 1.3 %conditional.2 = (f32[2,8,32]{2,1,0:T(8,128)S(1)}, f32[2,8,32,128]{3,2,1,0:T(8,128)S(1)}) conditional(s32[]{:T(128)} %bitcast.12, () %tuple.21, (s32[32]{0:T(128)S(1)}, bf16[64,16,128]{2,1,0:T(8,128)(2,1)S(1)}, bf16[512,2,128]{2,0,1:T(8,128)(2,1)S(1)}, bf16[512,2,128]{2,0,1:T(8,128)(2,1)S(1)}) %tuple.33), branch_computations={%region_0.1_spmd, %region_1.4_spmd} | conditional | flops 136592896 | bytes 4927632 | solution.py:80
  65.1 0.1 iota_compare_fusion
  65.1 0.4 fusion.26
  65.5 0.3 fusion.3
  65.9 0.4 fusion.4
  66.2 2.4 %collective-permute-done.7 = bf16[32,16,128]{2,1,0:T(8,128)(2,1)S(1)} collective-permute-done((bf16[32,16,128]{2,1,0:T(8,128)(2,1)S(1)}, bf16[32,16,128]{2,1,0:T(8,128)(2,1)S(1)}, u32[]{:S(2)}, u32[]{:S(2)}) %collective-permute-start.7) | collective-permute-done | bytes 131104 | tf_op jit(solution)/shard_map/ppermute | solution.py:8
  68.7 0.6 collective-permute-start.8
  69.3 0.1 fusion.24
  69.5 5.9 %collective-permute-done.8 = bf16[32,16,128]{2,1,0:T(8,128)(2,1)S(1)} collective-permute-done((bf16[32,16,128]{2,1,0:T(8,128)(2,1)S(1)}, bf16[32,16,128]{2,1,0:T(8,128)(2,1)S(1)}, u32[]{:S(2)}, u32[]{:S(2)}) %collective-permute-start.8) | collective-permute-done | bytes 131104 | tf_op jit(solution)/shard_map/ppermute | solution.py:8
  75.4 0.7 pad_maximum_fusion
  (31 shorter events, 0.4 us)
Async XLA Ops:
  0.0 0.9 %slice-start = ((bf16[64,16,128]{2,1,0:T(8,128)(2,1)}), bf16[32,16,128]{2,1,0:T(8,128)(2,1)S(1)}, s32[]{:S(2)}) async-start(bf16[64,16,128]{2,1,0:T(8,128)(2,1)} %param.7), calls=%async_computation | async-start | bytes 262144 | tf_op jit(solution)/shard_map/slice | solution.py:50
  0.9 3.1 %copy-start.1 = (bf16[64,2,128]{2,1,0:T(2,128)(2,1)S(1)}, bf16[64,2,128]{2,1,0:T(2,128)(2,1)}, u32[]{:S(2)}) copy-start(bf16[64,2,128]{2,1,0:T(2,128)(2,1)} %param.8) | copy-start | bytes 98308
  0.9 42.3 %collective-permute-start.3 = (bf16[32,16,128]{2,0,1:T(8,128)(2,1)S(1)}, bf16[32,16,128]{2,0,1:T(8,128)(2,1)S(1)}, u32[]{:S(2)}, u32[]{:S(2)}) collective-permute-start(bf16[32,16,128]{2,0,1:T(8,128)(2,1)S(1)} %copy.18), channel_id=1, source_target_pairs={{0,2},{2,0},{4,6},{6,4},{8,10},{10,8},{12,14},{14,12},{1,3},{3,1},... | collective-permute-start | bytes 393224 | tf_op jit(solution)/shard_map/ppermute | solution.py:8
  4.0 5.0 %copy-start.2 = (bf16[64,2,128]{2,1,0:T(2,128)(2,1)S(1)}, bf16[64,2,128]{2,1,0:T(2,128)(2,1)}, u32[]{:S(2)}) copy-start(bf16[64,2,128]{2,1,0:T(2,128)(2,1)} %param.9) | copy-start | bytes 98308
  4.0 5.3 %collective-permute-start = (bf16[64,2,128]{2,0,1:T(8,128)(2,1)S(1)}, bf16[64,2,128]{2,0,1:T(8,128)(2,1)S(1)}, u32[]{:S(2)}, u32[]{:S(2)}) collective-permute-start(bf16[64,2,128]{2,0,1:T(8,128)(2,1)S(1)} %get-tuple-element.48), channel_id=1, source_target_pairs={{0,14},{2,0},{4,2},{6,4},{8,6},{10,8},{12,10},{14,12},{1,15},{3,1}... | collective-permute-start | bytes 98312 | tf_op jit(solution)/shard_map/ppermute | solution.py:70
  9.4 33.8 %collective-permute-start.1 = (bf16[128,2,128]{2,0,1:T(8,128)(2,1)S(1)}, bf16[128,2,128]{2,0,1:T(8,128)(2,1)S(1)}, u32[]{:S(2)}, u32[]{:S(2)}) collective-permute-start(bf16[128,2,128]{2,0,1:T(8,128)(2,1)S(1)} %pad_maximum_fusion.2), channel_id=1, source_target_pairs={{0,12},{2,14},{4,0},{6,2},{8,4},{10,6},{12,8},{14,10},{1,13},{3,15... | collective-permute-start | bytes 196616 | tf_op jit(solution)/shard_map/ppermute | solution.py:70
  43.1 6.9 %collective-permute-start.2 = (bf16[256,2,128]{2,0,1:T(8,128)(2,1)S(1)}, bf16[256,2,128]{2,0,1:T(8,128)(2,1)S(1)}, u32[]{:S(2)}, u32[]{:S(2)}) collective-permute-start(bf16[256,2,128]{2,0,1:T(8,128)(2,1)S(1)} %pad_maximum_fusion.1), channel_id=1, source_target_pairs={{0,8},{2,10},{4,12},{6,14},{8,0},{10,2},{12,4},{14,6},{1,9},{3,11}... | collective-permute-start | bytes 393224 | tf_op jit(solution)/shard_map/ppermute | solution.py:70
  43.3 7.7 %collective-permute-start.4 = (bf16[32,16,128]{2,0,1:T(8,128)(2,1)S(1)}, bf16[32,16,128]{2,0,1:T(8,128)(2,1)S(1)}, u32[]{:S(2)}, u32[]{:S(2)}) collective-permute-start(bf16[32,16,128]{2,0,1:T(8,128)(2,1)S(1)} %collective-permute-done.3), channel_id=1, source_target_pairs={{0,4},{2,6},{4,0},{6,2},{8,12},{10,14},{12,8},{14,10},{1,5},{3,7},... | collective-permute-start | bytes 393224 | tf_op jit(solution)/shard_map/ppermute | solution.py:8
  51.0 6.3 %collective-permute-start.5 = (bf16[32,16,128]{2,0,1:T(8,128)(2,1)S(1)}, bf16[32,16,128]{2,0,1:T(8,128)(2,1)S(1)}, u32[]{:S(2)}, u32[]{:S(2)}) collective-permute-start(bf16[32,16,128]{2,0,1:T(8,128)(2,1)S(1)} %collective-permute-done.4), channel_id=1, source_target_pairs={{0,8},{2,10},{4,12},{6,14},{8,0},{10,2},{12,4},{14,6},{1,9},{3,11}... | collective-permute-start | bytes 393224 | tf_op jit(solution)/shard_map/ppermute | solution.py:8
  58.4 6.5 %copy-start = (bf16[64,16,128]{2,1,0:T(8,128)(2,1)S(1)}, bf16[64,16,128]{2,1,0:T(8,128)(2,1)}, u32[]{:S(2)}) copy-start(bf16[64,16,128]{2,1,0:T(8,128)(2,1)} %param.7) | copy-start | bytes 786436
  58.6 5.0 %collective-permute-start.6 = (bf16[32,16,128]{2,1,0:T(8,128)(2,1)S(1)}, bf16[32,16,128]{2,1,0:T(8,128)(2,1)S(1)}, u32[]{:S(2)}, u32[]{:S(2)}) collective-permute-start(bf16[32,16,128]{2,1,0:T(8,128)(2,1)S(1)} %bitcast.51), channel_id=1, source_target_pairs={{0,2},{2,0},{4,6},{6,4},{8,10},{10,8},{12,14},{14,12},{1,3},{3,1},... | collective-permute-start | bytes 393224 | tf_op jit(solution)/shard_map/ppermute | solution.py:8
  63.7 5.0 %collective-permute-start.7 = (bf16[32,16,128]{2,1,0:T(8,128)(2,1)S(1)}, bf16[32,16,128]{2,1,0:T(8,128)(2,1)S(1)}, u32[]{:S(2)}, u32[]{:S(2)}) collective-permute-start(bf16[32,16,128]{2,1,0:T(8,128)(2,1)S(1)} %collective-permute-done.6), channel_id=1, source_target_pairs={{0,4},{2,6},{4,0},{6,2},{8,12},{10,14},{12,8},{14,10},{1,5},{3,7},... | collective-permute-start | bytes 393224 | tf_op jit(solution)/shard_map/ppermute | solution.py:8
  68.7 6.7 %collective-permute-start.8 = (bf16[32,16,128]{2,1,0:T(8,128)(2,1)S(1)}, bf16[32,16,128]{2,1,0:T(8,128)(2,1)S(1)}, u32[]{:S(2)}, u32[]{:S(2)}) collective-permute-start(bf16[32,16,128]{2,1,0:T(8,128)(2,1)S(1)} %collective-permute-done.7), channel_id=1, source_target_pairs={{0,8},{2,10},{4,12},{6,14},{8,0},{10,2},{12,4},{14,6},{1,9},{3,11}... | collective-permute-start | bytes 393224 | tf_op jit(solution)/shard_map/ppermute | solution.py:8
